TPU v7x, 1024 devices: a whole 4x8x16 slice. The times are simulated.
1024 devices in a mesh: dom: 32 (over z, core), grp: 8 (over y), rep: 4 (over x).
Axes of the slice: x: 4, y: 8, z: 16, core: 2. Of those that a mesh axis runs over, the one named last changes fastest.
Arguments:
- features: bfloat16 [8192, 768], P(('rep', 'grp')), may hold values from -6 to 6
- tiles: bfloat16 [32, 4, 12, 256, 256], P('dom', 'rep', None, 'grp'), may hold values from 0 to 0.039794922
- columns: int32 [2, 32, 4, 8], replicated, may hold values from 0 to 7, as said below
- counts: int32 [2, 32, 4], replicated, may hold values from 1 to 8, as said below
- weights: bfloat16 [2, 768, 768], replicated, may hold values from -0.21875 to 0.21875
Outputs:
- aggregated: bfloat16 [8192, 768], P(('dom', 'grp', 'rep'))
Inputs may be any that keep to these rules, and one draw needn't show every extreme that they name: `columns`: within each list, the entries below the count name distinct source panels of the group; later entries are unused. An owner's two counts in a column group add up to 9 to 15, and 15 is reached; over all owners of a column group they add up to 384.
All inputs are finite; a program needn't handle non-finite values.
Results may differ from a plain program's by a relative error of at most 0.0085.
Values may be sent and summed in bfloat16 or wider, within the bound.
No kernel may reach another device: no remote copies, remote signals or barrier semaphores. Data moves between devices by JAX's collectives and lax.ppermute only.
A program may use at most 32 MiB of HBM per device.

v0:
```python
import jax
import jax.numpy as jnp
from jax import lax
from jax.sharding import PartitionSpec as P


def combine_rows(strips, panel_ids, labels, relation, present, panels, weights):
    chosen = jnp.take(panels, panel_ids, axis=0)
    products = jnp.einsum("kst,ktf->ksf", strips, chosen, preferred_element_type=jnp.float32)
    relation_kinds = jnp.arange(2, dtype=jnp.int32)
    member = (
        present[None, None, :]
        & (labels[:, None, None] == labels[None, None, :])
        & (relation[None, None, :] == relation_kinds[None, :, None])
    )
    group_sums = jnp.einsum(
        "krj,jsf->krsf", member.astype(jnp.float32), products, precision=lax.Precision.HIGHEST
    ).astype(jnp.bfloat16)
    mixed_rows = jnp.einsum(
        "krsf,rfg->ksg", group_sums, weights, preferred_element_type=jnp.float32
    ).astype(jnp.bfloat16)
    entry_index = jnp.arange(labels.shape[0], dtype=jnp.int32)
    earlier = (
        present[None, :]
        & (labels[:, None] == labels[None, :])
        & (entry_index[None, :] < entry_index[:, None])
    )
    leading = present & jnp.logical_not(jnp.any(earlier, axis=1))
    return (mixed_rows, leading)


def on_device(features, tiles, columns, counts, weights):
    slot_count = tiles.shape[2]
    strip_rows = tiles.shape[3]
    tile_cols = tiles.shape[4]
    list_len = columns.shape[3]
    feat_dim = features.shape[1]
    owners_count = lax.axis_size("dom")
    worker = lax.axis_index("dom")
    column_group = lax.axis_index("rep")
    gathered = lax.all_gather(features, "grp", axis=0, tiled=True)
    panels = gathered.reshape(list_len, tile_cols, feat_dim)
    strips = tiles.reshape(slot_count, strip_rows, tile_cols)
    first_counts = counts[0][:, column_group]
    group_loads = first_counts + counts[1][:, column_group]
    owner_ends = jnp.cumsum(group_loads)
    owner_starts = owner_ends - group_loads
    owner_range = jnp.arange(owners_count, dtype=jnp.int32)
    places = jnp.arange(slot_count, dtype=jnp.int32) * owners_count + worker
    slot_owner = jnp.sum((owner_ends[None, :] <= places[:, None]).astype(jnp.int32), axis=1)
    owner_hot = slot_owner[:, None] == owner_range[None, :]
    slot_start = jnp.sum(jnp.where(owner_hot, owner_starts[None, :], 0), axis=1)
    slot_first = jnp.sum(jnp.where(owner_hot, first_counts[None, :], 0), axis=1)
    offsets = places - slot_start
    slot_relation = (offsets >= slot_first).astype(jnp.int32)
    slot_entry = offsets - slot_relation * slot_first
    group_columns = columns[:, :, column_group, :]
    matches = (
        (slot_relation[:, None, None, None] == jnp.arange(2, dtype=jnp.int32)[None, :, None, None])
        & owner_hot[:, None, :, None]
        & (
            slot_entry[:, None, None, None]
            == jnp.arange(list_len, dtype=jnp.int32)[None, None, None, :]
        )
    )
    panel_ids = jnp.sum(jnp.where(matches, group_columns[None], 0), axis=(1, 2, 3))
    present_all = jnp.ones((slot_count,), dtype=jnp.bool_)
    mixed_rows, leading = combine_rows(
        strips, panel_ids, slot_owner, slot_relation, present_all, panels, weights
    )
    home_map = jnp.transpose(owner_hot) & leading[None, :]
    blocks = jnp.einsum(
        "dk,ksg->dsg", home_map.astype(jnp.bfloat16), mixed_rows, preferred_element_type=jnp.float32
    ).astype(jnp.bfloat16)
    returned = lax.all_to_all(blocks, "dom", split_axis=0, concat_axis=0, tiled=True)
    partial_value = jnp.sum(returned.astype(jnp.float32), axis=0)
    result = lax.psum_scatter(partial_value, "rep", scatter_dimension=0, tiled=True)
    return result.astype(jnp.bfloat16)


def solution(mesh):
    return jax.shard_map(
        on_device,
        mesh=mesh,
        in_specs=(P(("rep", "grp"), None), P("dom", "rep", None, "grp", None), P(), P(), P()),
        out_specs=P(("dom", "grp", "rep"), None),
        check_vma=False,
    )
```

profile of v0, /device:TPU:1, one launch (start us, length us, event | category | flops | bytes accessed | tf_op | source)
XLA Modules:
  0.0 203.3 jit_solution(5493765588964365762)
XLA Ops:
  6.5 0.7 all-gather.2.cloned.1.call-update
  7.3 0.7 fusion.37
  8.0 0.1 copy.15
  8.2 0.1 reduce
  8.3 0.2 convert_reduce_fusion.1
  8.5 0.2 fusion.26
  8.7 0.7 dynamic-slice_bitcast_fusion
  9.4 0.2 select_reduce_fusion.2
  9.6 0.1 iota_compare_fusion.2
  9.7 0.1 iota_compare_fusion.1
  9.7 0.1 iota_compare_fusion
  9.8 0.1 broadcast_and_fusion
  9.9 0.4 select_reduce_fusion
  10.3 60.2 %all-gather.2.cloned.1.call-done = bf16[2048,768]{1,0:T(8,128)(2,1)} async-done(((bf16[256,768]{1,0:T(8,128)(2,1)}), bf16[2048,768]{1,0:T(8,128)(2,1)}) %all-gather.2.cloned.1.call-update) | async-done | bytes 3145744 | tf_op jit(solution)/shard_map/all_gather | solution.py:41
  70.5 5.1 %gather_fusion = bf16[12,256,768]{2,1,0:T(8,128)(2,1)} fusion(bf16[8,256,768]{2,1,0:T(8,128)(2,1)} %bitcast.44, s32[1024]{0:T(1024)S(1)} %pad_clamp_fusion), kind=kCustom, calls=%fused_computation | custom fusion | bytes 9437232 | tf_op jit(solution)/shard_map/jit(_take)/gather | solution.py:8
  75.5 3.5 %fusion.11 = f32[12,32,768]{2,1,0:T(8,128)S(1)} fusion(bf16[12,256,768]{2,1,0:T(8,128)(2,1)} %gather_fusion, pred[12]{0:T(512)(128)(4,1)S(1)} %compare_and_fusion, bf16[1,1,12,32,256]{4,3,2,1,0:T(8,128)(2,1)S(1)} %copy-done.1), kind=kOutput, calls=%fused_computation.13 | convolution fusion | flops 153354240 | bytes 6094860 | tf_op jit(solution)/shard_map/kst,ktf->ksf/dot_general | solution.py:9
  79.0 1.9 convolution_convert_fusion.1
  81.0 1.3 fusion.14
  82.3 0.7 convolution_convert_fusion
  83.0 0.9 copy.19
  83.9 93.0 %all_to_all.5 = bf16[32,32,768]{2,1,0:T(8,128)(2,1)S(1)} all-to-all(bf16[32,32,768]{2,1,0:T(8,128)(2,1)S(1)} %copy.19), channel_id=1, replica_groups=mesh['dom'=32,'grp'=8,'rep'=4] {'dom'}, dimensions={0} | all-to-all | bytes 3145728 | tf_op jit(solution)/shard_map/all_to_all | solution.py:75
  176.9 0.8 convert_reduce_fusion
  177.8 17.4 %reduce-scatter.2.cloned.1.call-done = f32[8,768]{1,0:T(8,128)} async-done(((f32[32,768]{1,0:T(8,128)}), f32[8,768]{1,0:T(8,128)}) %reduce-scatter.2.cloned.1.call-update) | async-done | bytes 24592 | tf_op jit(solution)/shard_map/reduce_scatter | solution.py:77
  195.2 1.3 convert_element_type.37
  (18 shorter events, 0.2 us)
Async XLA Ops:
  6.5 74.4 %copy-start = (bf16[2,768,768]{2,1,0:T(8,128)(2,1)S(1)}, bf16[2,768,768]{2,1,0:T(8,128)(2,1)}, u32[]{:S(2)}) copy-start(bf16[2,768,768]{2,1,0:T(8,128)(2,1)} %param.9) | copy-start | bytes 7077892
  6.5 64.0 %all-gather.2.cloned.1.call-start = ((), (), s32[]{:S(2)}) async-start(), calls=%async_computation.2 | async-start | bytes 3538944 | tf_op jit(solution)/shard_map/all_gather | solution.py:41
  7.3 187.9 %reduce-scatter.2.cloned.1.call-start = ((), (), s32[]{:S(2)}) async-start(), calls=%async_computation.3 | async-start | bytes 122880 | tf_op jit(solution)/shard_map/reduce_scatter | solution.py:77
  70.5 5.1 %copy-start.1 = (bf16[1,1,12,32,256]{4,3,2,1,0:T(8,128)(2,1)S(1)}, bf16[1,1,12,32,256]{4,3,2,1,0:T(8,128)(2,1)}, u32[]{:S(2)}) copy-start(bf16[1,1,12,32,256]{4,3,2,1,0:T(8,128)(2,1)} %param.6) | copy-start | bytes 589828
Sparse Core Ops, SparseCore 0:
  10.0 60.4 all-gather.1
  177.9 17.1 reduce-scatter.1
where the time goes:
time: 205 us; the launch traced here: 203 us
  blocking collectives  93 us (45%)
  waiting for transfers between devices  78.2 us (38%)
  between operations  13.5 us (7%)
  matrix products  7.44 us (4%)
  local copies, waits for them, and re-layouts  7.42 us (4%)
  other arithmetic  3.65 us (2%)
    all_to_all x1, blocking collectives, on_device(): lax.all_to_all(blocks, 'dom', split_axis=0, concat_axis=0, tiled=True)  93 us
    all_gather x1, waiting for transfers between devices, on_device(): gathered = lax.all_gather(features, 'grp', axis=0, tiled=True)  60.2 us
    reduce_scatter x1, waiting for transfers between devices, on_device(): lax.psum_scatter(partial_value, 'rep', scatter_dimension=0, tiled=True)  17.4 us
    gather x1, local copies, waits for them, and re-layouts, combine_rows(): chosen = jnp.take(panels, panel_ids, axis=0)  5.05 us
  transfers between devices with their start and end apart: 2, of which 2 were waited for; matrix products, arithmetic and copies ran while one was open for 1% of the time, Pallas kernels for 0%

commit v1 on v0

v1 whole, which is shorter than its diff:
```python
import jax
import jax.numpy as jnp
from jax import lax
from jax.sharding import PartitionSpec as P


def on_device(features, tiles, columns, counts, weights):
    slot_count = tiles.shape[2]
    strip_rows = tiles.shape[3]
    tile_cols = tiles.shape[4]
    list_len = columns.shape[3]
    feat_dim = features.shape[1]
    owners_count = lax.axis_size("dom")
    me = lax.axis_index("dom")
    column_group = lax.axis_index("rep")
    max_load = 2 * list_len

    gathered = lax.all_gather(features, "grp", axis=0, tiled=True)
    panels = gathered.reshape(list_len * tile_cols, feat_dim)

    first_counts = counts[0][:, column_group]
    group_loads = first_counts + counts[1][:, column_group]
    owner_starts = jnp.cumsum(group_loads) - group_loads

    strips = tiles.reshape(slot_count, strip_rows, tile_cols)
    owner_slot = (owner_starts - me + owners_count - 1) // owners_count
    owner_slot = jnp.clip(owner_slot, 0, slot_count - 1)
    owner_place = me + owner_slot * owners_count
    owner_has = (owner_place >= owner_starts) & (owner_place < owner_starts + group_loads)
    outgoing = jnp.where(owner_has[:, None, None], jnp.take(strips, owner_slot, axis=0), jnp.zeros((), strips.dtype))
    incoming = lax.all_to_all(outgoing, "dom", split_axis=0, concat_axis=0, tiled=True)

    my_start = owner_starts[me]
    my_load = group_loads[me]
    my_first = first_counts[me]
    entry = jnp.arange(max_load, dtype=jnp.int32)
    entry_valid = entry < my_load
    entry_worker = (my_start + entry) % owners_count
    entry_rel = (entry >= my_first).astype(jnp.int32)
    entry_k = jnp.clip(entry - entry_rel * my_first, 0, list_len - 1)
    my_columns = columns[:, me, column_group, :]
    entry_col = my_columns[entry_rel, entry_k]
    blocks = jnp.take(incoming, entry_worker, axis=0)
    blocks = jnp.where(entry_valid[:, None, None], blocks, jnp.zeros((), blocks.dtype))
    col_hot = entry_col[:, None] == jnp.arange(list_len, dtype=jnp.int32)[None, :]
    placed = jnp.where(col_hot[:, None, :, None], blocks[:, :, None, :], jnp.zeros((), blocks.dtype))
    placed = placed.reshape(max_load * strip_rows, list_len * tile_cols)
    products = jnp.dot(placed, panels, preferred_element_type=jnp.float32).astype(jnp.bfloat16)
    products = products.reshape(max_load, strip_rows, feat_dim)
    rel_hot = entry_rel[:, None] == jnp.arange(2, dtype=jnp.int32)[None, :]
    split = jnp.where(rel_hot[:, None, :, None], products[:, :, None, :], jnp.zeros((), products.dtype))
    split = split.reshape(max_load * strip_rows, 2 * feat_dim)
    terms = jnp.dot(split, weights.reshape(2 * feat_dim, feat_dim), preferred_element_type=jnp.float32)
    terms = terms.astype(jnp.bfloat16).reshape(max_load, strip_rows, feat_dim)
    partial_value = jnp.sum(terms.astype(jnp.float32), axis=0)
    result = lax.psum_scatter(partial_value, "rep", scatter_dimension=0, tiled=True)
    return result.astype(jnp.bfloat16)


def solution(mesh):
    return jax.shard_map(
        on_device,
        mesh=mesh,
        in_specs=(P(("rep", "grp"), None), P("dom", "rep", None, "grp", None), P(), P(), P()),
        out_specs=P(("dom", "grp", "rep"), None),
        check_vma=False,
    )
```

time: 205 us -> 118 us (0.58)
  blocking collectives: 93 us -> 0 us
  starting transfers between devices: 0.04 us -> 20.4 us
  waiting for transfers between devices: 78.2 us -> 59.5 us
  other arithmetic: 3.65 us -> 8.61 us
    all_to_all x1 -> x0, blocking collectives: 93 us -> none  [on_device(): lax.all_to_all(blocks, 'dom', split_axis=0, concat_axis=0, tiled=True)]
    all_gather x1, waiting for transfers between devices: 60.2 us -> 2.75 us  [on_device(): gathered = lax.all_gather(features, 'grp', axis=0, tiled=True)]
    all_to_all x0 -> x1, waiting for transfers between devices: none -> 26.7 us  [on_device(): lax.all_to_all(outgoing, 'dom', split_axis=0, concat_axis=0, tiled=True)]
    all_to_all x0 -> x1, starting transfers between devices: none -> 20.4 us  [on_device(): lax.all_to_all(outgoing, 'dom', split_axis=0, concat_axis=0, tiled=True)]
    reduce_scatter x1, waiting for transfers between devices: 17.4 us -> 29.3 us  [on_device(): lax.psum_scatter(partial_value, 'rep', scatter_dimension=0, tiled=True)]
    select_n x1 -> x5, other arithmetic: 0.01 us -> 3.57 us  [the longest x1 1.66 us: on_device(): jnp.where(rel_hot[:, None, :, None], products[:, :, None, :], jnp.zeros((...]
    dynamic_slice x0 -> x4, local copies, waits for them, and re-layouts: none -> 2.74 us  [the longest x1 0.9 us: on_device(): my_columns = columns[:, me, column_group, :]]
    unnamed x4, local copies, waits for them, and re-layouts: 0.01 us -> 2.32 us
  transfers between devices with their start and end apart: 2 -> 3, of which waited for: 2 -> 3; matrix products, arithmetic and copies ran while one was open for 1% -> 11% of each run, Pallas kernels for 0% -> 0%
where the time goes in v1:
time: 118 us; the launch traced here: 116 us
  waiting for transfers between devices  59.5 us (50%)
  starting transfers between devices  20.4 us (17%)
  between operations  13.5 us (11%)
  other arithmetic  8.61 us (7%)
  local copies, waits for them, and re-layouts  8.6 us (7%)
  matrix products  5.68 us (5%)
    reduce_scatter x1, waiting for transfers between devices, on_device(): lax.psum_scatter(partial_value, 'rep', scatter_dimension=0, tiled=True)  29.3 us
    all_to_all x1, waiting for transfers between devices, on_device(): lax.all_to_all(outgoing, 'dom', split_axis=0, concat_axis=0, tiled=True)  26.7 us
    all_to_all x1, starting transfers between devices, on_device(): lax.all_to_all(outgoing, 'dom', split_axis=0, concat_axis=0, tiled=True)  20.4 us
    dot_general x1, matrix products, on_device(): jnp.dot(placed, panels, preferred_element_type=jnp.float32)  4.3 us
    all_gather x1, waiting for transfers between devices, on_device(): gathered = lax.all_gather(features, 'grp', axis=0, tiled=True)  2.75 us
  transfers between devices with their start and end apart: 3, of which 3 were waited for; matrix products, arithmetic and copies ran while one was open for 11% of the time, Pallas kernels for 0%

profile of v1, /device:TPU:1, one launch (start us, length us, event | category | flops | bytes accessed | tf_op | source)
XLA Modules:
  0.0 116.4 jit_solution(966770979915956905)
XLA Ops:
  6.5 0.7 all-gather.2.cloned.1.call-update
  7.3 0.7 fusion.19
  8.3 1.5 %gather_fusion.1 = bf16[32,32,256]{2,1,0:T(8,128)(2,1)S(1)} fusion(bf16[12,32,256]{2,1,0:T(8,128)(2,1)} %bitcast.31, s32[1024]{0:T(1024)S(1)} %pad_clamp_fusion.1), kind=kCustom, calls=%fused_computation.1 | custom fusion | bytes 1048704 | tf_op jit(solution)/shard_map/jit(_take)/gather | solution.py:30
  9.8 0.9 select_select_fusion
  10.7 20.4 %all-to-all-start = ((bf16[32,32,256]{2,1,0:T(8,128)(2,1)}), bf16[32,32,256]{2,1,0:T(8,128)(2,1)S(1)}, u32[]{:S(2)}, u32[]{:S(2)}) async-start(bf16[32,32,256]{2,1,0:T(8,128)(2,1)} %select_select_fusion), calls=%async_computation | async-start | bytes 1048576 | tf_op jit(solution)/shard_map/all_to_all | solution.py:31
  31.2 0.7 constant_dynamic-slice_fusion
  31.9 0.6 dynamic_slice.23
  32.5 0.6 constant_dynamic-slice_fusion.3
  33.0 0.9 dynamic-slice_reduce_fusion
  33.9 0.7 fusion.9
  34.6 0.7 gather_fusion
  35.3 0.7 compare_convert_fusion
  36.0 0.6 fusion.15
  36.5 1.3 %compare_and_fusion.2 = (pred[16]{0:T(512)(128)(4,1)S(1)}, pred[16]{0:T(512)(128)(4,1)S(1)}) fusion(s32[]{:T(128)} %bitcast.5, s32[]{:T(128)} %bitcast.2), kind=kLoop, calls=%fused_computation.39 | loop fusion | flops 304 | bytes 40 | tf_op jit(solution)/shard_map/jit(_take)/and | solution.py:43
  38.0 26.7 %all-to-all-done = bf16[32,32,256]{2,1,0:T(8,128)(2,1)S(1)} async-done(((bf16[32,32,256]{2,1,0:T(8,128)(2,1)}), bf16[32,32,256]{2,1,0:T(8,128)(2,1)S(1)}, u32[]{:S(2)}, u32[]{:S(2)}) %all-to-all-start) | async-done | bytes 524320 | tf_op jit(solution)/shard_map/all_to_all | solution.py:31
  64.7 0.6 gather_fusion.2
  65.7 2.1 %copy.10 = bf16[64,8,8,256]{3,1,2,0:T(8,128)(2,1)} copy(bf16[64,8,8,256]{3,2,1,0:T(8,128)(2,1)S(1)} %bitcast.27) | data formatting | bytes 4194304
  67.7 2.8 %all-gather.2.cloned.1.call-done = bf16[2048,768]{1,0:T(8,128)(2,1)} async-done(((bf16[256,768]{1,0:T(8,128)(2,1)}), bf16[2048,768]{1,0:T(8,128)(2,1)}) %all-gather.2.cloned.1.call-update) | async-done | bytes 3145744 | tf_op jit(solution)/shard_map/all_gather | solution.py:18
  70.5 4.3 %convolution_convert_fusion = bf16[512,768]{1,0:T(8,128)(2,1)S(1)} fusion(bf16[512,2048]{1,0:T(8,128)(2,1)} %bitcast.29, bf16[2048,768]{1,0:T(8,128)(2,1)} %all-gather.2.cloned.1.call-done), kind=kOutput, calls=%fused_computation.6 | convolution fusion | flops 1611005952 | bytes 6029312 | tf_op jit(solution)/shard_map/dot_general | solution.py:48
  74.8 1.7 %broadcast_select_fusion = bf16[16,32,2,768]{3,2,1,0:T(2,128)(2,1)S(1)} fusion(pred[16,2]{1,0:T(8,128)(4,1)S(1)} %iota_compare_fusion.1, bf16[16,32,768]{2,1,0:T(8,128)(2,1)S(1)} %bitcast.33), kind=kLoop, calls=%fused_computation.3 | loop fusion | flops 786432 | bytes 2359328 | tf_op jit(solution)/shard_map/jit(_where)/select_n | solution.py:51
  76.7 1.4 %convolution_convert_fusion.1 = bf16[512,768]{1,0:T(8,128)(2,1)S(1)} fusion(bf16[512,1536]{1,0:T(8,128)(2,1)S(1)} %bitcast.30, bf16[1536,768]{1,0:T(8,128)(2,1)S(1)} %bitcast.26), kind=kOutput, calls=%fused_computation.7 | convolution fusion | flops 1208352768 | bytes 4718592 | tf_op jit(solution)/shard_map/dot_general | solution.py:53
  78.1 0.7 convert_reduce_fusion
  78.9 29.3 %reduce-scatter.2.cloned.1.call-done = f32[8,768]{1,0:T(8,128)} async-done(((f32[32,768]{1,0:T(8,128)}), f32[8,768]{1,0:T(8,128)}) %reduce-scatter.2.cloned.1.call-update) | async-done | bytes 24592 | tf_op jit(solution)/shard_map/reduce_scatter | solution.py:56
  108.2 1.3 %convert_element_type.36 = bf16[8,768]{1,0:T(8,128)(2,1)} convert(f32[8,768]{1,0:T(8,128)} %reduce-scatter.2.cloned.1.call-done) | non-fusion elementwise | flops 6144 | bytes 36864 | tf_op jit(solution)/shard_map/convert_element_type | solution.py:57
  (18 shorter events, 1.2 us)
Async XLA Ops:
  6.5 70.2 %copy-start = (bf16[2,768,768]{2,1,0:T(8,128)(2,1)S(1)}, bf16[2,768,768]{2,1,0:T(8,128)(2,1)}, u32[]{:S(2)}) copy-start(bf16[2,768,768]{2,1,0:T(8,128)(2,1)} %param.9) | copy-start | bytes 7077892
  6.5 64.0 %all-gather.2.cloned.1.call-start = ((), (), s32[]{:S(2)}) async-start(), calls=%async_computation.2 | async-start | bytes 3538944 | tf_op jit(solution)/shard_map/all_gather | solution.py:18
  10.7 53.9 %all-to-all-start = ((bf16[32,32,256]{2,1,0:T(8,128)(2,1)}), bf16[32,32,256]{2,1,0:T(8,128)(2,1)S(1)}, u32[]{:S(2)}, u32[]{:S(2)}) async-start(bf16[32,32,256]{2,1,0:T(8,128)(2,1)} %select_select_fusion), calls=%async_computation | async-start | bytes 1048576 | tf_op jit(solution)/shard_map/all_to_all | solution.py:31
  31.2 77.0 %reduce-scatter.2.cloned.1.call-start = ((), (), s32[]{:S(2)}) async-start(), calls=%async_computation.3 | async-start | bytes 122880 | tf_op jit(solution)/shard_map/reduce_scatter | solution.py:56
Sparse Core Ops, SparseCore 0:
  10.0 60.4 all-gather.1
  79.0 29.1 reduce-scatter.1

commit v2 on v1

--- a/solution.py
+++ b/solution.py
@@ -53,8 +53,10 @@
     terms = jnp.dot(split, weights.reshape(2 * feat_dim, feat_dim), preferred_element_type=jnp.float32)
     terms = terms.astype(jnp.bfloat16).reshape(max_load, strip_rows, feat_dim)
     partial_value = jnp.sum(terms.astype(jnp.float32), axis=0)
-    result = lax.psum_scatter(partial_value, "rep", scatter_dimension=0, tiled=True)
-    return result.astype(jnp.bfloat16)
+    rep_count = lax.axis_size("rep")
+    pieces = partial_value.reshape(rep_count, strip_rows // rep_count, feat_dim)
+    pieces = lax.all_to_all(pieces, "rep", split_axis=0, concat_axis=0, tiled=True)
+    return jnp.sum(pieces, axis=0).astype(jnp.bfloat16)
 
 
 def solution(mesh):

time: 118 us -> 95.4 us (0.81)
  waiting for transfers between devices: 59.5 us -> 30.2 us
  blocking collectives: 0 us -> 8.44 us
  other arithmetic: 8.61 us -> 7.26 us
    reduce_scatter x1 -> x0, waiting for transfers between devices: 29.3 us -> none  [on_device(): lax.psum_scatter(partial_value, 'rep', scatter_dimension=0, tiled=True)]
    all_to_all x0 -> x1, blocking collectives: none -> 8.44 us  [on_device(): lax.all_to_all(pieces, 'rep', split_axis=0, concat_axis=0, tiled=True)]
    convert_element_type x1 -> x0, other arithmetic: 1.34 us -> none  [on_device(): return result.astype(jnp.bfloat16)]
  transfers between devices with their start and end apart: 3 -> 2, of which waited for: 3 -> 2; matrix products, arithmetic and copies ran while one was open for 11% -> 14% of each run, Pallas kernels for 0% -> 0%
where the time goes in v2:
time: 95.4 us; the launch traced here: 94.1 us
  waiting for transfers between devices  30.2 us (32%)
  starting transfers between devices  20.4 us (21%)
  between operations  13.5 us (14%)
  local copies, waits for them, and re-layouts  8.6 us (9%)
  blocking collectives  8.44 us (9%)
  other arithmetic  7.26 us (8%)
  matrix products  5.68 us (6%)
    all_to_all x1, waiting for transfers between devices, on_device(): lax.all_to_all(outgoing, 'dom', split_axis=0, concat_axis=0, tiled=True)  26.8 us
    all_to_all x1, starting transfers between devices, on_device(): lax.all_to_all(outgoing, 'dom', split_axis=0, concat_axis=0, tiled=True)  20.4 us
    all_to_all x1, blocking collectives, on_device(): lax.all_to_all(pieces, 'rep', split_axis=0, concat_axis=0, tiled=True)  8.44 us
    dot_general x1, matrix products, on_device(): jnp.dot(placed, panels, preferred_element_type=jnp.float32)  4.3 us
    all_gather x1, waiting for transfers between devices, on_device(): gathered = lax.all_gather(features, 'grp', axis=0, tiled=True)  2.74 us
    unnamed x4, local copies, waits for them, and re-layouts  2.32 us
  transfers between devices with their start and end apart: 2, of which 2 were waited for; matrix products, arithmetic and copies ran while one was open for 14% of the time, Pallas kernels for 0%

profile of v2, /device:TPU:1, one launch (start us, length us, event | category | flops | bytes accessed | tf_op | source)
XLA Modules:
  0.0 94.1 jit_solution(15786593881798119)
XLA Ops:
  6.5 0.7 all-gather.2.cloned.1.call-update
  7.3 0.7 fusion.19
  8.3 1.5 %gather_fusion.1 = bf16[32,32,256]{2,1,0:T(8,128)(2,1)S(1)} fusion(bf16[12,32,256]{2,1,0:T(8,128)(2,1)} %bitcast.32, s32[1024]{0:T(1024)S(1)} %pad_clamp_fusion.1), kind=kCustom, calls=%fused_computation.1 | custom fusion | bytes 1048704 | tf_op jit(solution)/shard_map/jit(_take)/gather | solution.py:30
  9.8 0.9 select_select_fusion
  10.7 20.4 %all-to-all-start = ((bf16[32,32,256]{2,1,0:T(8,128)(2,1)}), bf16[32,32,256]{2,1,0:T(8,128)(2,1)S(1)}, u32[]{:S(2)}, u32[]{:S(2)}) async-start(bf16[32,32,256]{2,1,0:T(8,128)(2,1)} %select_select_fusion), calls=%async_computation | async-start | bytes 1048576 | tf_op jit(solution)/shard_map/all_to_all | solution.py:31
  31.2 0.7 constant_dynamic-slice_fusion
  31.8 0.6 dynamic_slice.23
  32.4 0.6 constant_dynamic-slice_fusion.3
  33.0 0.9 dynamic-slice_reduce_fusion
  33.9 0.7 fusion.9
  34.6 0.7 gather_fusion
  35.3 0.7 compare_convert_fusion
  35.9 0.6 fusion.15
  36.5 1.3 %compare_and_fusion.2 = (pred[16]{0:T(512)(128)(4,1)S(1)}, pred[16]{0:T(512)(128)(4,1)S(1)}) fusion(s32[]{:T(128)} %bitcast.5, s32[]{:T(128)} %bitcast.2), kind=kLoop, calls=%fused_computation.39 | loop fusion | flops 304 | bytes 40 | tf_op jit(solution)/shard_map/jit(_take)/and | solution.py:43
  37.9 26.8 %all-to-all-done = bf16[32,32,256]{2,1,0:T(8,128)(2,1)S(1)} async-done(((bf16[32,32,256]{2,1,0:T(8,128)(2,1)}), bf16[32,32,256]{2,1,0:T(8,128)(2,1)S(1)}, u32[]{:S(2)}, u32[]{:S(2)}) %all-to-all-start) | async-done | bytes 524320 | tf_op jit(solution)/shard_map/all_to_all | solution.py:31
  64.7 0.6 gather_fusion.2
  65.4 0.3 broadcast_select_fusion.1
  65.7 2.1 %copy.12 = bf16[64,8,8,256]{3,1,2,0:T(8,128)(2,1)} copy(bf16[64,8,8,256]{3,2,1,0:T(8,128)(2,1)S(1)} %bitcast.28) | data formatting | bytes 4194304
  67.7 2.7 %all-gather.2.cloned.1.call-done = bf16[2048,768]{1,0:T(8,128)(2,1)} async-done(((bf16[256,768]{1,0:T(8,128)(2,1)}), bf16[2048,768]{1,0:T(8,128)(2,1)}) %all-gather.2.cloned.1.call-update) | async-done | bytes 3145744 | tf_op jit(solution)/shard_map/all_gather | solution.py:18
  70.5 4.3 %convolution_convert_fusion = bf16[512,768]{1,0:T(8,128)(2,1)S(1)} fusion(bf16[512,2048]{1,0:T(8,128)(2,1)} %bitcast.30, bf16[2048,768]{1,0:T(8,128)(2,1)} %all-gather.2.cloned.1.call-done), kind=kOutput, calls=%fused_computation.6 | convolution fusion | flops 1611005952 | bytes 6029312 | tf_op jit(solution)/shard_map/dot_general | solution.py:48
  74.8 1.7 %broadcast_select_fusion = bf16[16,32,2,768]{3,2,1,0:T(2,128)(2,1)S(1)} fusion(pred[16,2]{1,0:T(8,128)(4,1)S(1)} %iota_compare_fusion.1, bf16[16,32,768]{2,1,0:T(8,128)(2,1)S(1)} %bitcast.34), kind=kLoop, calls=%fused_computation.3 | loop fusion | flops 786432 | bytes 2359328 | tf_op jit(solution)/shard_map/jit(_where)/select_n | solution.py:51
  76.7 1.4 %convolution_convert_fusion.1 = bf16[512,768]{1,0:T(8,128)(2,1)S(1)} fusion(bf16[512,1536]{1,0:T(8,128)(2,1)S(1)} %bitcast.31, bf16[1536,768]{1,0:T(8,128)(2,1)S(1)} %bitcast.27), kind=kOutput, calls=%fused_computation.7 | convolution fusion | flops 1208352768 | bytes 4718592 | tf_op jit(solution)/shard_map/dot_general | solution.py:53
  78.2 8.4 %all_to_all.10 = f32[4,8,768]{2,1,0:T(8,128)S(1)} all-to-all(f32[4,8,768]{2,1,0:T(8,128)S(1)} %bitcast.35), channel_id=1, replica_groups=mesh['dom'=32,'grp'=8,'rep'=4] {'rep'}, dimensions={0} | all-to-all | bytes 196608 | tf_op jit(solution)/shard_map/all_to_all | solution.py:58
  86.7 0.6 reduce_sum.19
  (16 shorter events, 1.0 us)
Async XLA Ops:
  6.5 70.2 %copy-start = (bf16[2,768,768]{2,1,0:T(8,128)(2,1)S(1)}, bf16[2,768,768]{2,1,0:T(8,128)(2,1)}, u32[]{:S(2)}) copy-start(bf16[2,768,768]{2,1,0:T(8,128)(2,1)} %param.9) | copy-start | bytes 7077892
  6.5 63.9 %all-gather.2.cloned.1.call-start = ((), (), s32[]{:S(2)}) async-start(), calls=%async_computation.2 | async-start | bytes 3538944 | tf_op jit(solution)/shard_map/all_gather | solution.py:18
  10.7 53.9 %all-to-all-start = ((bf16[32,32,256]{2,1,0:T(8,128)(2,1)}), bf16[32,32,256]{2,1,0:T(8,128)(2,1)S(1)}, u32[]{:S(2)}, u32[]{:S(2)}) async-start(bf16[32,32,256]{2,1,0:T(8,128)(2,1)} %select_select_fusion), calls=%async_computation | async-start | bytes 1048576 | tf_op jit(solution)/shard_map/all_to_all | solution.py:31
Sparse Core Ops, SparseCore 0:
  10.0 60.4 all-gather.1

commit v3 on v2

--- a/solution.py
+++ b/solution.py
@@ -15,8 +15,33 @@
     column_group = lax.axis_index("rep")
     max_load = 2 * list_len
 
-    gathered = lax.all_gather(features, "grp", axis=0, tiled=True)
-    panels = gathered.reshape(list_len * tile_cols, feat_dim)
+    grp_count = lax.axis_size("grp")
+    my_grp = lax.axis_index("grp")
+    parity = me % 2
+    half = feat_dim // 2
+    mine = lax.dynamic_slice_in_dim(features, parity * half, half, axis=1)
+    up = [(i, (i + 1) % grp_count) for i in range(grp_count)]
+    down = [(i, (i - 1) % grp_count) for i in range(grp_count)]
+    pieces = [None] * grp_count
+    pieces[0] = mine
+    fwd = mine
+    bwd = mine
+    reach = grp_count // 2
+    for t in range(1, reach):
+        fwd = lax.ppermute(fwd, "grp", up)
+        bwd = lax.ppermute(bwd, "grp", down)
+        pieces[grp_count - t] = fwd
+        pieces[t] = bwd
+    rows_half = tile_cols // 2
+    far_a = lax.ppermute(fwd[:rows_half], "grp", up)
+    far_b = lax.ppermute(bwd[rows_half:], "grp", down)
+    pieces[reach] = jnp.concatenate([far_a, far_b], axis=0)
+    my_panels = jnp.stack(pieces, axis=0)
+    pairs = [(i, i ^ 1) for i in range(owners_count)]
+    other_panels = lax.ppermute(my_panels, "dom", pairs)
+    low = jnp.where(parity == 0, my_panels, other_panels)
+    high = jnp.where(parity == 0, other_panels, my_panels)
+    panels = jnp.concatenate([low, high], axis=2).reshape(list_len * tile_cols, feat_dim)
 
     first_counts = counts[0][:, column_group]
     group_loads = first_counts + counts[1][:, column_group]
@@ -39,7 +64,7 @@
     entry_rel = (entry >= my_first).astype(jnp.int32)
     entry_k = jnp.clip(entry - entry_rel * my_first, 0, list_len - 1)
     my_columns = columns[:, me, column_group, :]
-    entry_col = my_columns[entry_rel, entry_k]
+    entry_col = (my_columns[entry_rel, entry_k] - my_grp) % grp_count
     blocks = jnp.take(incoming, entry_worker, axis=0)
     blocks = jnp.where(entry_valid[:, None, None], blocks, jnp.zeros((), blocks.dtype))
     col_hot = entry_col[:, None] == jnp.arange(list_len, dtype=jnp.int32)[None, :]

time: 95.4 us -> 98 us (1.027)
  starting transfers between devices: 20.4 us -> 53.4 us
  waiting for transfers between devices: 30.2 us -> 7.87 us
  between operations: 13.5 us -> 0.31 us
  local copies, waits for them, and re-layouts: 8.6 us -> 13.9 us
  other arithmetic: 7.26 us -> 10 us
  matrix products: 5.68 us -> 3.18 us
    ppermute x0 -> x9, starting transfers between devices: none -> 33.6 us  [the longest x3 16.1 us: on_device(): bwd = lax.ppermute(bwd, 'grp', down)]
    all_to_all x1, waiting for transfers between devices: 26.8 us -> 0.01 us  [on_device(): lax.all_to_all(outgoing, 'dom', split_axis=0, concat_axis=0, tiled=True)]
    ppermute x0 -> x9, waiting for transfers between devices: none -> 7.87 us  [the longest x3 5.58 us: on_device(): fwd = lax.ppermute(fwd, 'grp', up)]
    unnamed x4 -> x12, local copies, waits for them, and re-layouts: 2.32 us -> 6.9 us
    all_gather x1 -> x0, waiting for transfers between devices: 2.74 us -> none  [on_device(): gathered = lax.all_gather(features, 'grp', axis=0, tiled=True)]
    dot_general x1, matrix products: 4.3 us -> 1.8 us  [on_device(): jnp.dot(placed, panels, preferred_element_type=jnp.float32)]
    select_n x0 -> x2, other arithmetic: none -> 1.71 us  [the longest x1 1.7 us: on_device(): low = jnp.where(parity == 0, my_panels, other_panels)]
  transfers between devices with their start and end apart: 2 -> 10, of which waited for: 2 -> 3; matrix products, arithmetic and copies ran while one was open for 14% -> 17% of each run, Pallas kernels for 0% -> 0%
where the time goes in v3:
time: 98 us; the launch traced here: 97.2 us
  starting transfers between devices  53.4 us (54%)
  local copies, waits for them, and re-layouts  13.9 us (14%)
  other arithmetic  10 us (10%)
  blocking collectives  8.48 us (9%)
  waiting for transfers between devices  7.87 us (8%)
  matrix products  3.18 us (3%)
    all_to_all x1, starting transfers between devices, on_device(): lax.all_to_all(outgoing, 'dom', split_axis=0, concat_axis=0, tiled=True)  19.9 us
    ppermute x3, starting transfers between devices, on_device(): bwd = lax.ppermute(bwd, 'grp', down)  16.1 us
    all_to_all x1, blocking collectives, on_device(): lax.all_to_all(pieces, 'rep', split_axis=0, concat_axis=0, tiled=True)  8.48 us
    unnamed x12, local copies, waits for them, and re-layouts  6.9 us
    ppermute x3, starting transfers between devices, on_device(): fwd = lax.ppermute(fwd, 'grp', up)  5.76 us
    ppermute x3, waiting for transfers between devices, on_device(): fwd = lax.ppermute(fwd, 'grp', up)  5.58 us
    ppermute x1, starting transfers between devices, on_device(): other_panels = lax.ppermute(my_panels, 'dom', pairs)  5.26 us
    ppermute x1, starting transfers between devices, on_device(): far_b = lax.ppermute(bwd[rows_half:], 'grp', down)  4.57 us
  transfers between devices with their start and end apart: 10, of which 3 were waited for; matrix products, arithmetic and copies ran while one was open for 17% of the time, Pallas kernels for 0%

profile of v3, /device:TPU:1, one launch (start us, length us, event | category | flops | bytes accessed | tf_op | source)
XLA Modules:
  0.0 97.2 jit_solution(11151047625003225419)
XLA Ops:
  0.0 1.8 %bitcast_dynamic-update-slice_fusion.6 = (bf16[8,256,384]{2,1,0:T(8,128)(2,1)}, bf16[256,384]{1,0:T(8,128)(2,1)S(1)}) fusion(bf16[256,768]{1,0:T(8,128)(2,1)} %param.5, s32[]{:T(128)S(6)} %select_n.208), kind=kLoop, calls=%fused_computation.21 | loop fusion | bytes 589828
  1.8 5.9 %collective-permute-start = (bf16[256,384]{1,0:T(8,128)(2,1)S(1)}, bf16[256,384]{1,0:T(8,128)(2,1)S(1)}, u32[]{:S(2)}, u32[]{:S(2)}) collective-permute-start(bf16[256,384]{1,0:T(8,128)(2,1)S(1)} %get-tuple-element.8), channel_id=1, source_target_pairs={{0,28},{4,0},{8,4},{12,8},{16,12},{20,16},{24,20},{28,24},{1,29},{... | collective-permute-start | bytes 589832 | tf_op jit(solution)/shard_map/ppermute | solution.py:32
  7.7 1.9 %collective-permute-start.3 = (bf16[256,384]{1,0:T(8,128)(2,1)S(1)}, bf16[256,384]{1,0:T(8,128)(2,1)S(1)}, u32[]{:S(2)}, u32[]{:S(2)}) collective-permute-start(bf16[256,384]{1,0:T(8,128)(2,1)S(1)} %get-tuple-element.8), channel_id=1, source_target_pairs={{0,4},{4,8},{8,12},{12,16},{16,20},{20,24},{24,28},{28,0},{1,5},{5... | collective-permute-start | bytes 589832 | tf_op jit(solution)/shard_map/ppermute | solution.py:31
  10.7 1.5 %gather_fusion.1 = bf16[32,32,256]{2,1,0:T(8,128)(2,1)S(1)} fusion(bf16[12,32,256]{2,1,0:T(8,128)(2,1)} %bitcast.52, s32[1024]{0:T(1024)S(1)} %pad_clamp_fusion.1), kind=kCustom, calls=%fused_computation.1 | custom fusion | bytes 1048704 | tf_op jit(solution)/shard_map/jit(_take)/gather | solution.py:55
  12.2 0.9 select_select_fusion
  13.1 19.9 %all-to-all-start = ((bf16[32,32,256]{2,1,0:T(8,128)(2,1)}), bf16[32,32,256]{2,1,0:T(8,128)(2,1)S(1)}, u32[]{:S(2)}, u32[]{:S(2)}) async-start(bf16[32,32,256]{2,1,0:T(8,128)(2,1)} %select_select_fusion), calls=%async_computation | async-start | bytes 1048576 | tf_op jit(solution)/shard_map/all_to_all | solution.py:56
  34.3 4.9 %collective-permute-start.1 = (bf16[256,384]{1,0:T(8,128)(2,1)S(1)}, bf16[256,384]{1,0:T(8,128)(2,1)S(1)}, u32[]{:S(2)}, u32[]{:S(2)}) collective-permute-start(bf16[256,384]{1,0:T(8,128)(2,1)S(1)} %collective-permute-done), channel_id=1, source_target_pairs={{0,28},{4,0},{8,4},{12,8},{16,12},{20,16},{24,20},{28,24},{1,29},{... | collective-permute-start | bytes 589832 | tf_op jit(solution)/shard_map/ppermute | solution.py:32
  39.1 1.9 %collective-permute-start.4 = (bf16[256,384]{1,0:T(8,128)(2,1)S(1)}, bf16[256,384]{1,0:T(8,128)(2,1)S(1)}, u32[]{:S(2)}, u32[]{:S(2)}) collective-permute-start(bf16[256,384]{1,0:T(8,128)(2,1)S(1)} %collective-permute-done.3), channel_id=1, source_target_pairs={{0,4},{4,8},{8,12},{12,16},{16,20},{20,24},{24,28},{28,0},{1,5},{5... | collective-permute-start | bytes 589832 | tf_op jit(solution)/shard_map/ppermute | solution.py:31
  41.8 1.4 %collective-permute-done.1 = bf16[256,384]{1,0:T(8,128)(2,1)S(1)} collective-permute-done((bf16[256,384]{1,0:T(8,128)(2,1)S(1)}, bf16[256,384]{1,0:T(8,128)(2,1)S(1)}, u32[]{:S(2)}, u32[]{:S(2)}) %collective-permute-start.1) | collective-permute-done | bytes 196640 | tf_op jit(solution)/shard_map/ppermute | solution.py:32
  43.1 5.3 %collective-permute-start.2 = (bf16[256,384]{1,0:T(8,128)(2,1)S(1)}, bf16[256,384]{1,0:T(8,128)(2,1)S(1)}, u32[]{:S(2)}, u32[]{:S(2)}) collective-permute-start(bf16[256,384]{1,0:T(8,128)(2,1)S(1)} %collective-permute-done.1), channel_id=1, source_target_pairs={{0,28},{4,0},{8,4},{12,8},{16,12},{20,16},{24,20},{28,24},{1,29},{... | collective-permute-start | bytes 589832 | tf_op jit(solution)/shard_map/ppermute | solution.py:32
  48.5 1.9 %collective-permute-start.5 = (bf16[256,384]{1,0:T(8,128)(2,1)S(1)}, bf16[256,384]{1,0:T(8,128)(2,1)S(1)}, u32[]{:S(2)}, u32[]{:S(2)}) collective-permute-start(bf16[256,384]{1,0:T(8,128)(2,1)S(1)} %collective-permute-done.4), channel_id=1, source_target_pairs={{0,4},{4,8},{8,12},{12,16},{16,20},{20,24},{24,28},{28,0},{1,5},{5... | collective-permute-start | bytes 589832 | tf_op jit(solution)/shard_map/ppermute | solution.py:31
  51.1 5.6 %collective-permute-done.5 = bf16[256,384]{1,0:T(8,128)(2,1)S(1)} collective-permute-done((bf16[256,384]{1,0:T(8,128)(2,1)S(1)}, bf16[256,384]{1,0:T(8,128)(2,1)S(1)}, u32[]{:S(2)}, u32[]{:S(2)}) %collective-permute-start.5) | collective-permute-done | bytes 196640 | tf_op jit(solution)/shard_map/ppermute | solution.py:31
  56.7 1.9 %collective-permute-start.6 = (bf16[128,384]{1,0:T(8,128)(2,1)S(1)}, bf16[128,384]{1,0:T(8,128)(2,1)S(1)}, u32[]{:S(2)}, u32[]{:S(2)}) collective-permute-start(bf16[128,384]{1,0:T(8,128)(2,1)S(1)} %slice.22), channel_id=1, source_target_pairs={{0,4},{4,8},{8,12},{12,16},{16,20},{20,24},{24,28},{28,0},{1,5},{5... | collective-permute-start | bytes 294920 | tf_op jit(solution)/shard_map/ppermute | solution.py:36
  58.6 4.6 %collective-permute-start.7 = (bf16[128,384]{1,0:T(8,128)(2,1)S(1)}, bf16[128,384]{1,0:T(8,128)(2,1)S(1)}, u32[]{:S(2)}, u32[]{:S(2)}) collective-permute-start(bf16[128,384]{1,0:T(8,128)(2,1)S(1)} %slice.23), channel_id=1, source_target_pairs={{0,28},{4,0},{8,4},{12,8},{16,12},{20,16},{24,20},{28,24},{1,29},{... | collective-permute-start | bytes 294920 | tf_op jit(solution)/shard_map/ppermute | solution.py:37
  63.9 0.9 collective-permute-done.7
  66.9 0.7 bitcast_dynamic-update-slice_fusion
  67.6 5.3 %collective-permute-start.8 = (bf16[8,256,384]{2,1,0:T(8,128)(2,1)}, bf16[8,256,384]{2,1,0:T(8,128)(2,1)}, u32[]{:S(2)}, u32[]{:S(2)}) collective-permute-start(bf16[8,256,384]{2,1,0:T(8,128)(2,1)} %bitcast_dynamic-update-slice_fusion), channel_id=1, source_target_pairs={{0,32},{32,0},{64,96},{96,64},{128,160},{160,128},{192,224},{224,1... | collective-permute-start | bytes 4718600 | tf_op jit(solution)/shard_map/ppermute | solution.py:41
  74.8 0.9 dynamic-slice_reduce_fusion
  77.0 1.3 %compare_and_fusion.2 = (pred[16]{0:T(512)(128)(4,1)S(1)}, pred[16]{0:T(512)(128)(4,1)S(1)}) fusion(s32[]{:T(128)} %bitcast.5, s32[]{:T(128)} %bitcast.2), kind=kLoop, calls=%fused_computation.53 | loop fusion | flops 304 | bytes 40 | tf_op jit(solution)/shard_map/jit(_take)/and | solution.py:68
  80.9 1.7 %broadcast_select_fusion.3 = (bf16[8,256,384]{2,1,0:T(8,128)(2,1)S(1)}, bf16[8,256,384]{2,1,0:T(8,128)(2,1)S(1)}) fusion(bf16[8,256,384]{2,1,0:T(8,128)(2,1)S(1)} %copy-done.1, bf16[8,256,384]{2,1,0:T(8,128)(2,1)} %collective-permute-done.8, pred[]{:T(512)S(6)} %eq.49), kind=kLoop, calls=%fused_computation.8 | loop fusion | flops 1572864 | bytes 6291457 | tf_op jit(solution)/shard_map/jit(_where)/select_n | solution.py:42
  82.9 1.8 %convolution_convert_fusion = bf16[512,768]{1,0:T(8,128)(2,1)S(1)} fusion(bf16[512,2048]{1,0:T(8,128)(2,1)S(1)} %bitcast.50, bf16[2048,768]{1,0:T(8,128)(2,1)S(1)} %bitcast.49), kind=kOutput, calls=%fused_computation.9 | convolution fusion | flops 1611005952 | bytes 6029312 | tf_op jit(solution)/shard_map/dot_general | solution.py:73
  84.7 1.7 %broadcast_select_fusion = bf16[16,32,2,768]{3,2,1,0:T(2,128)(2,1)S(1)} fusion(pred[16,2]{1,0:T(8,128)(4,1)S(1)} %iota_compare_fusion.1, bf16[16,32,768]{2,1,0:T(8,128)(2,1)S(1)} %bitcast.54), kind=kLoop, calls=%fused_computation.4 | loop fusion | flops 786432 | bytes 2359328 | tf_op jit(solution)/shard_map/jit(_where)/select_n | solution.py:76
  86.7 1.4 %convolution_convert_fusion.1 = bf16[512,768]{1,0:T(8,128)(2,1)S(1)} fusion(bf16[512,1536]{1,0:T(8,128)(2,1)S(1)} %bitcast.51, bf16[1536,768]{1,0:T(8,128)(2,1)S(1)} %bitcast.46), kind=kOutput, calls=%fused_computation.10 | convolution fusion | flops 1208352768 | bytes 4718592 | tf_op jit(solution)/shard_map/dot_general | solution.py:78
  88.2 8.5 %all_to_all.10 = f32[4,8,768]{2,1,0:T(8,128)S(1)} all-to-all(f32[4,8,768]{2,1,0:T(8,128)S(1)} %bitcast.55), channel_id=1, replica_groups=mesh['dom'=32,'grp'=8,'rep'=4] {'rep'}, dimensions={0} | all-to-all | bytes 196608 | tf_op jit(solution)/shard_map/all_to_all | solution.py:83
  (46 shorter events, 13.5 us)
Async XLA Ops:
  0.0 86.7 %copy-start = (bf16[2,768,768]{2,1,0:T(8,128)(2,1)S(1)}, bf16[2,768,768]{2,1,0:T(8,128)(2,1)}, u32[]{:S(2)}) copy-start(bf16[2,768,768]{2,1,0:T(8,128)(2,1)} %param.9) | copy-start | bytes 7077892
  1.8 32.5 %collective-permute-start = (bf16[256,384]{1,0:T(8,128)(2,1)S(1)}, bf16[256,384]{1,0:T(8,128)(2,1)S(1)}, u32[]{:S(2)}, u32[]{:S(2)}) collective-permute-start(bf16[256,384]{1,0:T(8,128)(2,1)S(1)} %get-tuple-element.8), channel_id=1, source_target_pairs={{0,28},{4,0},{8,4},{12,8},{16,12},{20,16},{24,20},{28,24},{1,29},{... | collective-permute-start | bytes 589832 | tf_op jit(solution)/shard_map/ppermute | solution.py:32
  7.7 31.4 %collective-permute-start.3 = (bf16[256,384]{1,0:T(8,128)(2,1)S(1)}, bf16[256,384]{1,0:T(8,128)(2,1)S(1)}, u32[]{:S(2)}, u32[]{:S(2)}) collective-permute-start(bf16[256,384]{1,0:T(8,128)(2,1)S(1)} %get-tuple-element.8), channel_id=1, source_target_pairs={{0,4},{4,8},{8,12},{12,16},{16,20},{20,24},{24,28},{28,0},{1,5},{5... | collective-permute-start | bytes 589832 | tf_op jit(solution)/shard_map/ppermute | solution.py:31
  13.1 65.4 %all-to-all-start = ((bf16[32,32,256]{2,1,0:T(8,128)(2,1)}), bf16[32,32,256]{2,1,0:T(8,128)(2,1)S(1)}, u32[]{:S(2)}, u32[]{:S(2)}) async-start(bf16[32,32,256]{2,1,0:T(8,128)(2,1)} %select_select_fusion), calls=%async_computation | async-start | bytes 1048576 | tf_op jit(solution)/shard_map/all_to_all | solution.py:56
  34.3 8.9 %collective-permute-start.1 = (bf16[256,384]{1,0:T(8,128)(2,1)S(1)}, bf16[256,384]{1,0:T(8,128)(2,1)S(1)}, u32[]{:S(2)}, u32[]{:S(2)}) collective-permute-start(bf16[256,384]{1,0:T(8,128)(2,1)S(1)} %collective-permute-done), channel_id=1, source_target_pairs={{0,28},{4,0},{8,4},{12,8},{16,12},{20,16},{24,20},{28,24},{1,29},{... | collective-permute-start | bytes 589832 | tf_op jit(solution)/shard_map/ppermute | solution.py:32
  39.1 9.3 %collective-permute-start.4 = (bf16[256,384]{1,0:T(8,128)(2,1)S(1)}, bf16[256,384]{1,0:T(8,128)(2,1)S(1)}, u32[]{:S(2)}, u32[]{:S(2)}) collective-permute-start(bf16[256,384]{1,0:T(8,128)(2,1)S(1)} %collective-permute-done.3), channel_id=1, source_target_pairs={{0,4},{4,8},{8,12},{12,16},{16,20},{20,24},{24,28},{28,0},{1,5},{5... | collective-permute-start | bytes 589832 | tf_op jit(solution)/shard_map/ppermute | solution.py:31
  43.1 15.5 %collective-permute-start.2 = (bf16[256,384]{1,0:T(8,128)(2,1)S(1)}, bf16[256,384]{1,0:T(8,128)(2,1)S(1)}, u32[]{:S(2)}, u32[]{:S(2)}) collective-permute-start(bf16[256,384]{1,0:T(8,128)(2,1)S(1)} %collective-permute-done.1), channel_id=1, source_target_pairs={{0,28},{4,0},{8,4},{12,8},{16,12},{20,16},{24,20},{28,24},{1,29},{... | collective-permute-start | bytes 589832 | tf_op jit(solution)/shard_map/ppermute | solution.py:32
  48.5 8.2 %collective-permute-start.5 = (bf16[256,384]{1,0:T(8,128)(2,1)S(1)}, bf16[256,384]{1,0:T(8,128)(2,1)S(1)}, u32[]{:S(2)}, u32[]{:S(2)}) collective-permute-start(bf16[256,384]{1,0:T(8,128)(2,1)S(1)} %collective-permute-done.4), channel_id=1, source_target_pairs={{0,4},{4,8},{8,12},{12,16},{16,20},{20,24},{24,28},{28,0},{1,5},{5... | collective-permute-start | bytes 589832 | tf_op jit(solution)/shard_map/ppermute | solution.py:31
  56.7 7.3 %collective-permute-start.6 = (bf16[128,384]{1,0:T(8,128)(2,1)S(1)}, bf16[128,384]{1,0:T(8,128)(2,1)S(1)}, u32[]{:S(2)}, u32[]{:S(2)}) collective-permute-start(bf16[128,384]{1,0:T(8,128)(2,1)S(1)} %slice.22), channel_id=1, source_target_pairs={{0,4},{4,8},{8,12},{12,16},{16,20},{20,24},{24,28},{28,0},{1,5},{5... | collective-permute-start | bytes 294920 | tf_op jit(solution)/shard_map/ppermute | solution.py:36
  58.6 6.2 %collective-permute-start.7 = (bf16[128,384]{1,0:T(8,128)(2,1)S(1)}, bf16[128,384]{1,0:T(8,128)(2,1)S(1)}, u32[]{:S(2)}, u32[]{:S(2)}) collective-permute-start(bf16[128,384]{1,0:T(8,128)(2,1)S(1)} %slice.23), channel_id=1, source_target_pairs={{0,28},{4,0},{8,4},{12,8},{16,12},{20,16},{24,20},{28,24},{1,29},{... | collective-permute-start | bytes 294920 | tf_op jit(solution)/shard_map/ppermute | solution.py:37
  67.6 12.6 %collective-permute-start.8 = (bf16[8,256,384]{2,1,0:T(8,128)(2,1)}, bf16[8,256,384]{2,1,0:T(8,128)(2,1)}, u32[]{:S(2)}, u32[]{:S(2)}) collective-permute-start(bf16[8,256,384]{2,1,0:T(8,128)(2,1)} %bitcast_dynamic-update-slice_fusion), channel_id=1, source_target_pairs={{0,32},{32,0},{64,96},{96,64},{128,160},{160,128},{192,224},{224,1... | collective-permute-start | bytes 4718600 | tf_op jit(solution)/shard_map/ppermute | solution.py:41
  79.5 1.4 %copy-start.1 = (bf16[8,256,384]{2,1,0:T(8,128)(2,1)S(1)}, bf16[8,256,384]{2,1,0:T(8,128)(2,1)}, u32[]{:S(2)}) copy-start(bf16[8,256,384]{2,1,0:T(8,128)(2,1)} %bitcast_dynamic-update-slice_fusion) | copy-start | bytes 4718596

commit v4 on v2

--- a/solution.py
+++ b/solution.py
@@ -10,25 +10,40 @@
     tile_cols = tiles.shape[4]
     list_len = columns.shape[3]
     feat_dim = features.shape[1]
-    owners_count = lax.axis_size("dom")
-    me = lax.axis_index("dom")
+    chip_count = lax.axis_size("z")
+    core_count = lax.axis_size("core")
+    owners_count = chip_count * core_count
+    my_core = lax.axis_index("core")
+    me = lax.axis_index("z") * core_count + my_core
     column_group = lax.axis_index("rep")
     max_load = 2 * list_len
 
-    gathered = lax.all_gather(features, "grp", axis=0, tiled=True)
-    panels = gathered.reshape(list_len * tile_cols, feat_dim)
+    swap = [(0, 1), (1, 0)]
+    half = feat_dim // core_count
+    mine = lax.dynamic_slice_in_dim(features, my_core * half, half, axis=1)
+    mine = lax.all_gather(mine, "grp", axis=0, tiled=True)
+    other = lax.ppermute(mine, "core", swap)
+    low = jnp.where(my_core == 0, mine, other)
+    high = jnp.where(my_core == 0, other, mine)
+    panels = jnp.concatenate([low, high], axis=1)
 
     first_counts = counts[0][:, column_group]
     group_loads = first_counts + counts[1][:, column_group]
     owner_starts = jnp.cumsum(group_loads) - group_loads
 
     strips = tiles.reshape(slot_count, strip_rows, tile_cols)
-    owner_slot = (owner_starts - me + owners_count - 1) // owners_count
-    owner_slot = jnp.clip(owner_slot, 0, slot_count - 1)
-    owner_place = me + owner_slot * owners_count
-    owner_has = (owner_place >= owner_starts) & (owner_place < owner_starts + group_loads)
-    outgoing = jnp.where(owner_has[:, None, None], jnp.take(strips, owner_slot, axis=0), jnp.zeros((), strips.dtype))
-    incoming = lax.all_to_all(outgoing, "dom", split_axis=0, concat_axis=0, tiled=True)
+    chip_loads = group_loads.reshape(chip_count, core_count).sum(axis=1)
+    chip_starts = owner_starts.reshape(chip_count, core_count)[:, 0]
+    chip_slot = (chip_starts - me + owners_count - 1) // owners_count
+    chip_slot = jnp.clip(chip_slot, 0, slot_count - 1)
+    chip_place = me + chip_slot * owners_count
+    chip_has = (chip_place >= chip_starts) & (chip_place < chip_starts + chip_loads)
+    outgoing = jnp.where(chip_has[:, None, None], jnp.take(strips, chip_slot, axis=0), jnp.zeros((), strips.dtype))
+    from_chips = lax.all_to_all(outgoing, "z", split_axis=0, concat_axis=0, tiled=True)
+    from_sibling = lax.ppermute(from_chips, "core", swap)
+    from_core0 = jnp.where(my_core == 0, from_chips, from_sibling)
+    from_core1 = jnp.where(my_core == 0, from_sibling, from_chips)
+    incoming = jnp.stack([from_core0, from_core1], axis=1).reshape(owners_count, strip_rows, tile_cols)
 
     my_start = owner_starts[me]
     my_load = group_loads[me]
@@ -60,10 +75,14 @@
 
 
 def solution(mesh):
+    dom_size, grp_size, rep_size = mesh.devices.shape
+    split = jax.sharding.Mesh(
+        mesh.devices.reshape(dom_size // 2, 2, grp_size, rep_size), ("z", "core", "grp", "rep")
+    )
     return jax.shard_map(
         on_device,
-        mesh=mesh,
-        in_specs=(P(("rep", "grp"), None), P("dom", "rep", None, "grp", None), P(), P(), P()),
-        out_specs=P(("dom", "grp", "rep"), None),
+        mesh=split,
+        in_specs=(P(("rep", "grp"), None), P(("z", "core"), "rep", None, "grp", None), P(), P(), P()),
+        out_specs=P(("z", "core", "grp", "rep"), None),
         check_vma=False,
     )

time: 95.4 us -> 103 us (1.080)
  starting transfers between devices: 20.4 us -> 28.1 us
  other arithmetic: 7.26 us -> 10.3 us
  matrix products: 5.68 us -> 3.17 us
  waiting for transfers between devices: 30.2 us -> 28.3 us
  local copies, waits for them, and re-layouts: 8.6 us -> 10.4 us
    all_to_all x1, waiting for transfers between devices: 26.8 us -> 0.01 us  [on_device(): lax.all_to_all(outgoing, 'z', split_axis=0, concat_axis=0, tiled=True)]
    all_gather x1, waiting for transfers between devices: 2.74 us -> 28.3 us  [on_device(): mine = lax.all_gather(mine, 'grp', axis=0, tiled=True)]
    ppermute x0 -> x2, starting transfers between devices: none -> 8.72 us  [the longest x1 6.8 us: on_device(): other = lax.ppermute(mine, 'core', swap)]
    dot_general x1, matrix products: 4.3 us -> 1.79 us  [on_device(): jnp.dot(placed, panels, preferred_element_type=jnp.float32)]
    dynamic_slice x0 -> x1, local copies, waits for them, and re-layouts: none -> 1.76 us  [on_device(): mine = lax.dynamic_slice_in_dim(features, my_core * half, half, axis=1)]
    select_n x1 -> x3, other arithmetic: 0.93 us -> 2.65 us  [the longest x1 1.7 us: on_device(): low = jnp.where(my_core == 0, mine, other)]
    unnamed x4 -> x6, local copies, waits for them, and re-layouts: 2.32 us -> 1.64 us
  transfers between devices with their start and end apart: 2 -> 4, of which waited for: 2 -> 1; matrix products, arithmetic and copies ran while one was open for 14% -> 14% of each run, Pallas kernels for 0% -> 0%
where the time goes in v4:
time: 103 us; the launch traced here: 102 us
  waiting for transfers between devices  28.3 us (27%)
  starting transfers between devices  28.1 us (27%)
  between operations  13.6 us (13%)
  local copies, waits for them, and re-layouts  10.4 us (10%)
  other arithmetic  10.3 us (10%)
  blocking collectives  8.43 us (8%)
  matrix products  3.17 us (3%)
    all_gather x1, waiting for transfers between devices, on_device(): mine = lax.all_gather(mine, 'grp', axis=0, tiled=True)  28.3 us
    all_to_all x1, starting transfers between devices, on_device(): lax.all_to_all(outgoing, 'z', split_axis=0, concat_axis=0, tiled=True)  19.4 us
    all_to_all x1, blocking collectives, on_device(): lax.all_to_all(pieces, 'rep', split_axis=0, concat_axis=0, tiled=True)  8.43 us
    ppermute x1, starting transfers between devices, on_device(): other = lax.ppermute(mine, 'core', swap)  6.8 us
  transfers between devices with their start and end apart: 4, of which 1 were waited for; matrix products, arithmetic and copies ran while one was open for 14% of the time, Pallas kernels for 0%

profile of v4, /device:TPU:1, one launch (start us, length us, event | category | flops | bytes accessed | tf_op | source)
XLA Modules:
  0.0 102.3 jit_solution(7560568472549405533)
XLA Ops:
  6.5 1.8 %constant_dynamic-slice_fusion = bf16[256,384]{1,0:T(8,128)(2,1)} fusion(bf16[256,768]{1,0:T(8,128)(2,1)} %param.5, s32[]{:T(128)S(6)} %select_n.182), kind=kLoop, calls=%fused_computation.63 | loop fusion | bytes 393220 | tf_op jit(solution)/shard_map/dynamic_slice | solution.py:23
  8.3 0.7 fusion.27
  9.6 0.7 fusion.25
  11.1 1.5 %gather_fusion.1 = bf16[16,32,256]{2,1,0:T(8,128)(2,1)S(1)} fusion(bf16[12,32,256]{2,1,0:T(8,128)(2,1)} %bitcast.36, s32[1024]{0:T(1024)S(1)} %pad_clamp_fusion.1), kind=kCustom, calls=%fused_computation.1 | custom fusion | bytes 524352 | tf_op jit(solution)/shard_map/jit(_take)/gather | solution.py:41
  12.7 0.8 select_select_fusion.1
  13.5 19.4 %all-to-all-start = ((bf16[16,32,256]{2,1,0:T(8,128)(2,1)}), bf16[16,32,256]{2,1,0:T(8,128)(2,1)S(1)}, u32[]{:S(2)}, u32[]{:S(2)}) async-start(bf16[16,32,256]{2,1,0:T(8,128)(2,1)} %select_select_fusion.1), calls=%async_computation | async-start | bytes 524288 | tf_op jit(solution)/shard_map/all_to_all | solution.py:42
  33.5 28.3 %all-gather.2.cloned.1.call-done = bf16[2048,384]{1,0:T(8,128)(2,1)} async-done(((bf16[256,384]{1,0:T(8,128)(2,1)}), bf16[2048,384]{1,0:T(8,128)(2,1)}) %all-gather.2.cloned.1.call-update) | async-done | bytes 1572880 | tf_op jit(solution)/shard_map/all_gather | solution.py:24
  61.8 6.8 %collective-permute-start.1 = (bf16[2048,384]{1,0:T(8,128)(2,1)}, bf16[2048,384]{1,0:T(8,128)(2,1)}, u32[]{:S(2)}, u32[]{:S(2)}) collective-permute-start(bf16[2048,384]{1,0:T(8,128)(2,1)} %all-gather.2.cloned.1.call-done), channel_id=1, source_target_pairs={{0,32},{32,0},{1,33},{33,1},{2,34},{34,2},{3,35},{35,3},{4,36},{36... | collective-permute-start | bytes 4718600 | tf_op jit(solution)/shard_map/ppermute | solution.py:25
  68.6 0.7 compare_convert_fusion
  69.3 0.7 constant_dynamic-slice_fusion.1
  70.5 0.7 fusion.16
  71.3 1.9 %collective-permute-start = (bf16[16,32,256]{2,1,0:T(8,128)(2,1)S(1)}, bf16[16,32,256]{2,1,0:T(8,128)(2,1)S(1)}, u32[]{:S(2)}, u32[]{:S(2)}) collective-permute-start(bf16[16,32,256]{2,1,0:T(8,128)(2,1)S(1)} %all-to-all-done), channel_id=1, source_target_pairs={{0,32},{32,0},{1,33},{33,1},{2,34},{34,2},{3,35},{35,3},{4,36},{36... | collective-permute-start | bytes 786440 | tf_op jit(solution)/shard_map/ppermute | solution.py:43
  73.2 1.3 %compare_and_fusion.1 = (pred[16]{0:T(512)(128)(4,1)S(1)}, pred[16]{0:T(512)(128)(4,1)S(1)}) fusion(s32[]{:T(128)} %bitcast.4, s32[]{:T(128)} %bitcast.1), kind=kLoop, calls=%fused_computation.60 | loop fusion | flops 304 | bytes 40 | tf_op jit(solution)/shard_map/jit(_take)/and | solution.py:58
  74.5 0.9 dynamic-slice_reduce_fusion
  75.4 0.8 fusion.13
  76.2 0.7 gather_fusion
  78.1 0.7 copy.11
  78.8 0.7 copy-done.1
  79.5 1.7 %broadcast_select_fusion.3 = (bf16[2048,384]{1,0:T(8,128)(2,1)S(1)}, bf16[2048,384]{1,0:T(8,128)(2,1)S(1)}) fusion(bf16[2048,384]{1,0:T(8,128)(2,1)S(1)} %copy-done.1, bf16[2048,384]{1,0:T(8,128)(2,1)} %collective-permute-done.1, pred[]{:T(512)S(6)} %eq.48), kind=kLoop, calls=%fused_computation.11 | loop fusion | flops 1572864 | bytes 6291457 | tf_op jit(solution)/shard_map/jit(_where)/select_n | solution.py:26
  81.2 1.8 %fusion.4 = bf16[512,768]{1,0:T(8,128)(2,1)S(1)} fusion(bf16[512,2048]{1,0:T(8,128)(2,1)S(1)} %bitcast.30, bf16[2048,384]{1,0:T(8,128)(2,1)S(1)} %get-tuple-element.10, bf16[2048,384]{1,0:T(8,128)(2,1)S(1)} %get-tuple-element.9), kind=kOutput, calls=%fused_computation.12 | convolution fusion | flops 1617297408 | bytes 6029312 | tf_op jit(solution)/shard_map/dot_general | solution.py:63
  83.0 1.7 %broadcast_select_fusion = bf16[16,32,2,768]{3,2,1,0:T(2,128)(2,1)S(1)} fusion(pred[16,2]{1,0:T(8,128)(4,1)S(1)} %iota_compare_fusion.2, bf16[16,32,768]{2,1,0:T(8,128)(2,1)S(1)} %bitcast.34), kind=kLoop, calls=%fused_computation.7 | loop fusion | flops 786432 | bytes 2359328 | tf_op jit(solution)/shard_map/jit(_where)/select_n | solution.py:66
  85.0 1.4 %convolution_convert_fusion = bf16[512,768]{1,0:T(8,128)(2,1)S(1)} fusion(bf16[512,1536]{1,0:T(8,128)(2,1)S(1)} %bitcast.31, bf16[1536,768]{1,0:T(8,128)(2,1)S(1)} %bitcast.27), kind=kOutput, calls=%fused_computation.13 | convolution fusion | flops 1208352768 | bytes 4718592 | tf_op jit(solution)/shard_map/dot_general | solution.py:68
  86.5 8.4 %all_to_all.10 = f32[4,8,768]{2,1,0:T(8,128)S(1)} all-to-all(f32[4,8,768]{2,1,0:T(8,128)S(1)} %bitcast.35), channel_id=1, replica_groups=mesh['z'=16,'core'=2,'grp'=8,'rep'=4] {'rep'}, dimensions={0} | all-to-all | bytes 196608 | tf_op jit(solution)/shard_map/all_to_all | solution.py:73
  94.9 0.6 reduce_sum.29
  (34 shorter events, 4.3 us)
Async XLA Ops:
  6.5 78.4 %copy-start = (bf16[2,768,768]{2,1,0:T(8,128)(2,1)S(1)}, bf16[2,768,768]{2,1,0:T(8,128)(2,1)}, u32[]{:S(2)}) copy-start(bf16[2,768,768]{2,1,0:T(8,128)(2,1)} %param.9) | copy-start | bytes 7077892
  6.5 55.3 %all-gather.2.cloned.1.call-start = ((), (), s32[]{:S(2)}) async-start(), calls=%async_computation.2 | async-start | bytes 1769472 | tf_op jit(solution)/shard_map/all_gather | solution.py:24
  13.5 57.8 %all-to-all-start = ((bf16[16,32,256]{2,1,0:T(8,128)(2,1)}), bf16[16,32,256]{2,1,0:T(8,128)(2,1)S(1)}, u32[]{:S(2)}, u32[]{:S(2)}) async-start(bf16[16,32,256]{2,1,0:T(8,128)(2,1)} %select_select_fusion.1), calls=%async_computation | async-start | bytes 524288 | tf_op jit(solution)/shard_map/all_to_all | solution.py:42
  61.8 17.0 %collective-permute-start.1 = (bf16[2048,384]{1,0:T(8,128)(2,1)}, bf16[2048,384]{1,0:T(8,128)(2,1)}, u32[]{:S(2)}, u32[]{:S(2)}) collective-permute-start(bf16[2048,384]{1,0:T(8,128)(2,1)} %all-gather.2.cloned.1.call-done), channel_id=1, source_target_pairs={{0,32},{32,0},{1,33},{33,1},{2,34},{34,2},{3,35},{35,3},{4,36},{36... | collective-permute-start | bytes 4718600 | tf_op jit(solution)/shard_map/ppermute | solution.py:25
  71.3 5.6 %collective-permute-start = (bf16[16,32,256]{2,1,0:T(8,128)(2,1)S(1)}, bf16[16,32,256]{2,1,0:T(8,128)(2,1)S(1)}, u32[]{:S(2)}, u32[]{:S(2)}) collective-permute-start(bf16[16,32,256]{2,1,0:T(8,128)(2,1)S(1)} %all-to-all-done), channel_id=1, source_target_pairs={{0,32},{32,0},{1,33},{33,1},{2,34},{34,2},{3,35},{35,3},{4,36},{36... | collective-permute-start | bytes 786440 | tf_op jit(solution)/shard_map/ppermute | solution.py:43
  78.1 1.4 %copy-start.1 = (bf16[2048,384]{1,0:T(8,128)(2,1)S(1)}, bf16[2048,384]{1,0:T(8,128)(2,1)}, u32[]{:S(2)}) copy-start(bf16[2048,384]{1,0:T(8,128)(2,1)} %all-gather.2.cloned.1.call-done) | copy-start | bytes 4718596
Sparse Core Ops, SparseCore 0:
  10.0 51.7 all-gather.1

commit v5 on v2

--- a/solution.py
+++ b/solution.py
@@ -42,15 +42,16 @@
     entry_col = my_columns[entry_rel, entry_k]
     blocks = jnp.take(incoming, entry_worker, axis=0)
     blocks = jnp.where(entry_valid[:, None, None], blocks, jnp.zeros((), blocks.dtype))
-    col_hot = entry_col[:, None] == jnp.arange(list_len, dtype=jnp.int32)[None, :]
-    placed = jnp.where(col_hot[:, None, :, None], blocks[:, :, None, :], jnp.zeros((), blocks.dtype))
-    placed = placed.reshape(max_load * strip_rows, list_len * tile_cols)
+    rows = max_load * strip_rows
+    row_col = jnp.repeat(entry_col, strip_rows)
+    lane_panel = jnp.arange(list_len * tile_cols, dtype=jnp.int32) // tile_cols
+    placed = jnp.tile(blocks.reshape(rows, tile_cols), (1, list_len))
+    placed = jnp.where(row_col[:, None] == lane_panel[None, :], placed, jnp.zeros((), placed.dtype))
     products = jnp.dot(placed, panels, preferred_element_type=jnp.float32).astype(jnp.bfloat16)
-    products = products.reshape(max_load, strip_rows, feat_dim)
-    rel_hot = entry_rel[:, None] == jnp.arange(2, dtype=jnp.int32)[None, :]
-    split = jnp.where(rel_hot[:, None, :, None], products[:, :, None, :], jnp.zeros((), products.dtype))
-    split = split.reshape(max_load * strip_rows, 2 * feat_dim)
-    terms = jnp.dot(split, weights.reshape(2 * feat_dim, feat_dim), preferred_element_type=jnp.float32)
+    row_rel = jnp.repeat(entry_rel, strip_rows)[:, None]
+    zero = jnp.zeros((), products.dtype)
+    terms = jnp.dot(jnp.where(row_rel == 0, products, zero), weights[0], preferred_element_type=jnp.float32)
+    terms = terms + jnp.dot(jnp.where(row_rel == 1, products, zero), weights[1], preferred_element_type=jnp.float32)
     terms = terms.astype(jnp.bfloat16).reshape(max_load, strip_rows, feat_dim)
     partial_value = jnp.sum(terms.astype(jnp.float32), axis=0)
     rep_count = lax.axis_size("rep")

time: 95.4 us -> 93.4 us (0.979)
  local copies, waits for them, and re-layouts: 8.6 us -> 7.12 us
  other arithmetic: 7.26 us -> 5.82 us
  waiting for transfers between devices: 30.2 us -> 31.2 us
    all_gather x1, waiting for transfers between devices: 2.74 us -> 4.98 us  [on_device(): gathered = lax.all_gather(features, 'grp', axis=0, tiled=True)]
    select_n x2 -> x1, other arithmetic: 1.97 us -> 0.01 us  [on_device(): lane_panel = jnp.arange(list_len * tile_cols, dtype=jnp.int32) // tile_cols]
    unnamed x4 -> x5, local copies, waits for them, and re-layouts: 2.32 us -> 0.69 us
    all_to_all x1, waiting for transfers between devices: 26.8 us -> 25.5 us  [on_device(): lax.all_to_all(outgoing, 'dom', split_axis=0, concat_axis=0, tiled=True)]
  transfers between devices with their start and end apart: 2 -> 2, of which waited for: 2 -> 2; matrix products, arithmetic and copies ran while one was open for 14% -> 13% of each run, Pallas kernels for 0% -> 0%
where the time goes in v5:
time: 93.4 us; the launch traced here: 92.1 us
  waiting for transfers between devices  31.2 us (33%)
  starting transfers between devices  20.4 us (22%)
  between operations  13.5 us (14%)
  blocking collectives  8.4 us (9%)
  local copies, waits for them, and re-layouts  7.12 us (8%)
  other arithmetic  5.82 us (6%)
  matrix products  5.59 us (6%)
    all_to_all x1, waiting for transfers between devices, on_device(): lax.all_to_all(outgoing, 'dom', split_axis=0, concat_axis=0, tiled=True)  25.5 us
    all_to_all x1, starting transfers between devices, on_device(): lax.all_to_all(outgoing, 'dom', split_axis=0, concat_axis=0, tiled=True)  20.4 us
    all_to_all x1, blocking collectives, on_device(): lax.all_to_all(pieces, 'rep', split_axis=0, concat_axis=0, tiled=True)  8.4 us
    all_gather x1, waiting for transfers between devices, on_device(): gathered = lax.all_gather(features, 'grp', axis=0, tiled=True)  4.98 us
    dot_general x1, matrix products, on_device(): jnp.dot(placed, panels, preferred_element_type=jnp.float32)  3.9 us
  transfers between devices with their start and end apart: 2, of which 2 were waited for; matrix products, arithmetic and copies ran while one was open for 13% of the time, Pallas kernels for 0%

profile of v5, /device:TPU:1, one launch (start us, length us, event | category | flops | bytes accessed | tf_op | source)
XLA Modules:
  0.0 92.1 jit_solution(13643788650572663880)
XLA Ops:
  6.5 0.7 all-gather.2.cloned.1.call-update
  7.3 0.7 fusion.44
  8.3 0.6 gather_fusion.1
  8.9 0.9 %select_select_fusion = bf16[32,32,256]{2,1,0:T(8,128)(2,1)} fusion(bf16[32,32,256]{2,1,0:T(8,128)(2,1)S(1)} %gather_fusion.1, pred[32]{0:T(512)(128)(4,1)S(1)} %compare_and_fusion, pred[32]{0:T(512)(128)(4,1)S(1)} %get-tuple-element.7), kind=kLoop, calls=%fused_computation.20 | loop fusion | flops 524288 | bytes 1048640 | tf_op jit(solution)/shard_map/jit(_where)/select_n | solution.py:30
  9.8 20.4 %all-to-all-start = ((bf16[32,32,256]{2,1,0:T(8,128)(2,1)}), bf16[32,32,256]{2,1,0:T(8,128)(2,1)S(1)}, u32[]{:S(2)}, u32[]{:S(2)}) async-start(bf16[32,32,256]{2,1,0:T(8,128)(2,1)} %select_select_fusion), calls=%async_computation | async-start | bytes 1048576 | tf_op jit(solution)/shard_map/all_to_all | solution.py:31
  30.2 0.7 constant_dynamic-slice_fusion
  30.9 0.6 dynamic_slice.23
  31.5 0.6 constant_dynamic-slice_fusion.3
  32.1 1.2 %compare_and_fusion.2 = (pred[16]{0:T(512)(128)(4,1)S(1)}, pred[16]{0:T(512)(128)(4,1)S(1)}) fusion(s32[]{:T(128)} %bitcast.5, s32[]{:T(128)} %bitcast), kind=kLoop, calls=%fused_computation.59 | loop fusion | flops 336 | bytes 40 | tf_op jit(solution)/shard_map/jit(_take)/and | solution.py:43
  33.5 0.7 iota_compare_fusion
  34.3 0.9 dynamic-slice_reduce_fusion
  35.2 0.6 fusion.29
  35.8 0.7 gather_fusion
  36.8 0.6 fusion.37
  37.6 0.7 fusion.35
  38.3 25.5 %all-to-all-done = bf16[32,32,256]{2,1,0:T(8,128)(2,1)S(1)} async-done(((bf16[32,32,256]{2,1,0:T(8,128)(2,1)}), bf16[32,32,256]{2,1,0:T(8,128)(2,1)S(1)}, u32[]{:S(2)}, u32[]{:S(2)}) %all-to-all-start) | async-done | bytes 524320 | tf_op jit(solution)/shard_map/all_to_all | solution.py:31
  63.8 0.6 gather_fusion.2
  64.8 0.7 copy.12
  65.5 5.0 %all-gather.2.cloned.1.call-done = bf16[2048,768]{1,0:T(8,128)(2,1)} async-done(((bf16[256,768]{1,0:T(8,128)(2,1)}), bf16[2048,768]{1,0:T(8,128)(2,1)}) %all-gather.2.cloned.1.call-update) | async-done | bytes 3145744 | tf_op jit(solution)/shard_map/all_gather | solution.py:18
  70.5 3.9 %fusion.3 = bf16[512,768]{1,0:T(8,128)(2,1)S(1)} fusion(bf16[2048,768]{1,0:T(8,128)(2,1)} %all-gather.2.cloned.1.call-done, bf16[512,2048]{1,0:T(8,128)(2,1)S(1)} %bitcast.30, s32[2048]{0:T(1024)S(1)} %add_select_fusion.1, s32[512]{0:T(512)S(1)} %eq.50), kind=kOutput, calls=%fused_computation.9 | convolution fusion | flops 1613103104 | bytes 6039552 | tf_op jit(solution)/shard_map/dot_general | solution.py:50
  74.4 0.8 fusion.5
  75.3 0.8 add_convert_fusion
  76.2 8.4 %all_to_all.10 = f32[4,8,768]{2,1,0:T(8,128)S(1)} all-to-all(f32[4,8,768]{2,1,0:T(8,128)S(1)} %bitcast.32), channel_id=1, replica_groups=mesh['dom'=32,'grp'=8,'rep'=4] {'rep'}, dimensions={0} | all-to-all | bytes 196608 | tf_op jit(solution)/shard_map/all_to_all | solution.py:59
  84.6 0.6 reduce_sum.19
  (27 shorter events, 1.7 us)
Async XLA Ops:
  6.5 1.7 %copy-start = (bf16[1,1,12,32,256]{4,3,2,1,0:T(8,128)(2,1)S(1)}, bf16[1,1,12,32,256]{4,3,2,1,0:T(8,128)(2,1)}, u32[]{:S(2)}) copy-start(bf16[1,1,12,32,256]{4,3,2,1,0:T(8,128)(2,1)} %param.6) | copy-start | bytes 589828
  6.5 64.0 %all-gather.2.cloned.1.call-start = ((), (), s32[]{:S(2)}) async-start(), calls=%async_computation.2 | async-start | bytes 3538944 | tf_op jit(solution)/shard_map/all_gather | solution.py:18
  9.8 53.9 %all-to-all-start = ((bf16[32,32,256]{2,1,0:T(8,128)(2,1)}), bf16[32,32,256]{2,1,0:T(8,128)(2,1)S(1)}, u32[]{:S(2)}, u32[]{:S(2)}) async-start(bf16[32,32,256]{2,1,0:T(8,128)(2,1)} %select_select_fusion), calls=%async_computation | async-start | bytes 1048576 | tf_op jit(solution)/shard_map/all_to_all | solution.py:31
  70.5 3.9 %copy-start.1 = (bf16[2,768,768]{2,1,0:T(8,128)(2,1)S(1)}, bf16[2,768,768]{2,1,0:T(8,128)(2,1)}, u32[]{:S(2)}) copy-start(bf16[2,768,768]{2,1,0:T(8,128)(2,1)} %param.9) | copy-start | bytes 7077892
Sparse Core Ops, SparseCore 0:
  10.0 60.4 all-gather.1
